TPU v7x, 256 devices: a whole 4x4x8 slice. The times are simulated.
256 devices in a mesh: win: 32 (over y, z), grp: 8 (over x, core).
Axes of the slice: x: 4, y: 4, z: 8, core: 2. Of those that a mesh axis runs over, the one named last changes fastest.
Arguments:
- points: bfloat16 [32, 8, 512, 512], P('win', 'grp'), may hold values from -6 to 6
- rank: int32 [32, 8, 512], P('win', 'grp'), may hold values from 0 to 16383, as said below
- counts: int32 [8, 32, 8], replicated, may hold values from 1 to 128, 512 in all within a row
- w_qkv_one: bfloat16 [512, 1536], replicated
- w_out_one: bfloat16 [512, 512], replicated, may hold values from -0.25 to 0.25
- w_up: bfloat16 [512, 2048], replicated, may hold values from -0.25 to 0.25
- w_down: bfloat16 [2048, 512], replicated, may hold values from -0.125 to 0.125
- w_qkv_two: bfloat16 [512, 1536], replicated
- w_out_two: bfloat16 [512, 512], replicated, may hold values from -0.25 to 0.25
Outputs:
- encoded: bfloat16 [32, 8, 512, 512], P('win', 'grp')
Inputs may be any that keep to these rules, and one draw needn't show every extreme that they name: Within each of the 8 grp columns, rank over all 32 devices of win is a permutation of 0 to 16383. Each device holds at most 32 points whose rank // 512 is any one owner, and exactly 32 for some owner; each owner receives exactly 32 from some device. For each grp column and owner the 8 counts sum to 512, and the largest is 128.
All inputs are finite; a program needn't handle non-finite values.
Results may differ from a plain program's by a relative error of at most 0.03.
The roundings to bfloat16 on the way count: a program that leaves them out, or rounds other values in their place, can miss the bound.
Values may be sent and summed in bfloat16 or wider, within the bound.
No kernel may reach another device: no remote copies, remote signals or barrier semaphores. Data moves between devices by JAX's collectives and lax.ppermute only.
A program may use at most 128 MiB of HBM per device.

v0:
```python
import jax
import jax.numpy as jnp
from jax import lax
from jax.sharding import PartitionSpec as P

HEAD_DIM = 32
WINDOW_SLOTS = 128
EPSILON = 1e-05
MASKED = -1e30
SLOT_BASE = 32
TAIL = 128


def normalize(row_data):
    values = row_data.astype(jnp.float32)
    center = values - jnp.mean(values, axis=-1, keepdims=True)
    spread = jnp.mean(center * center, axis=-1, keepdims=True)
    return (center * lax.rsqrt(spread + EPSILON)).astype(jnp.bfloat16)


def project(row_data, weight):
    return jnp.dot(normalize(row_data), weight, preferred_element_type=jnp.float32).astype(
        jnp.bfloat16
    )


def attention_block(row_data, valid, w_qkv, w_out):
    rows_count, model_dim = row_data.shape
    heads_count = model_dim // HEAD_DIM
    block_count = rows_count // WINDOW_SLOTS
    normed = normalize(row_data)
    w_split = w_qkv.reshape(model_dim, 3, heads_count, HEAD_DIM)

    def head_major(part):
        out = jnp.einsum(
            "nd,dhe->hne", normed, w_split[:, part], preferred_element_type=jnp.float32
        )
        return out.astype(jnp.bfloat16).reshape(heads_count, block_count, WINDOW_SLOTS, HEAD_DIM)

    query, key, value = (head_major(0), head_major(1), head_major(2))
    scores = jnp.einsum(
        "hbqe,hbke->hbqk", query, key, preferred_element_type=jnp.float32
    ) * HEAD_DIM ** (-0.5)
    scores = jnp.where(valid[None, :, None, :], scores, MASKED)
    row_max = jnp.max(scores, axis=-1, keepdims=True)
    weights = jnp.exp(scores - row_max)
    weights = (weights / jnp.sum(weights, axis=-1, keepdims=True)).astype(jnp.bfloat16)
    context = jnp.einsum("hbqk,hbke->hbqe", weights, value, preferred_element_type=jnp.float32)
    context = context.astype(jnp.bfloat16).reshape(heads_count, rows_count, HEAD_DIM)
    mixed = jnp.einsum(
        "hne,hed->nd",
        context,
        w_out.reshape(heads_count, HEAD_DIM, model_dim),
        preferred_element_type=jnp.float32,
    )
    return (row_data.astype(jnp.float32) + mixed).astype(jnp.bfloat16)


def feed_forward(row_data, w_up, w_down):
    hidden = jax.nn.gelu(
        jnp.dot(normalize(row_data), w_up, preferred_element_type=jnp.float32), approximate=True
    ).astype(jnp.bfloat16)
    return (
        row_data.astype(jnp.float32) + jnp.dot(hidden, w_down, preferred_element_type=jnp.float32)
    ).astype(jnp.bfloat16)


def place(onehot, rows):
    return jnp.dot(onehot, rows, preferred_element_type=jnp.float32).astype(jnp.bfloat16)


def place_back(onehot, rows):
    return lax.dot_general(
        onehot, rows, (((0,), (0,)), ((), ())), preferred_element_type=jnp.float32
    ).astype(jnp.bfloat16)


def on_device(points, rank, counts, w_qkv_one, w_out_one, w_up, w_down, w_qkv_two, w_out_two):
    owner_count = lax.axis_size("win")
    group_count = lax.axis_size("grp")
    win_index = lax.axis_index("win")
    grp_index = lax.axis_index("grp")
    local_points = points.shape[2]
    model_dim = points.shape[3]
    blocks = counts.shape[2]
    slots_all = blocks * WINDOW_SLOTS
    capacity = 2 * local_points // owner_count
    buffer_rows = owner_count * capacity
    dilation_stride = WINDOW_SLOTS // group_count
    rows_x = points.reshape(local_points, model_dim)
    point_rank = rank.reshape(local_points)
    column_counts = lax.dynamic_index_in_dim(counts, grp_index, 0, keepdims=False)
    owner_dev = lax.div(point_rank, local_points)
    owner_ids = jnp.arange(owner_count, dtype=jnp.int32)
    choose = (owner_dev[:, None] == owner_ids[None, :]).astype(jnp.int32)
    point_ids = jnp.arange(local_points, dtype=jnp.int32)
    lower = (point_ids[None, :] <= point_ids[:, None]).astype(jnp.bfloat16)
    running = jnp.dot(lower, choose.astype(jnp.bfloat16), preferred_element_type=jnp.float32)
    peer_order = jnp.sum(choose * (running.astype(jnp.int32) - 1), axis=1)
    send_place = owner_dev * capacity + peer_order
    buffer_ids = jnp.arange(buffer_rows, dtype=jnp.int32)
    send_hot = (buffer_ids[:, None] == send_place[None, :]).astype(jnp.bfloat16)
    window_ends = jnp.cumsum(column_counts, axis=1)
    starts = window_ends - column_counts
    offset = lax.rem(point_rank, local_points)
    table = jnp.concatenate(
        [
            lax.div(window_ends, SLOT_BASE),
            lax.rem(window_ends, SLOT_BASE),
            lax.div(starts, SLOT_BASE),
            lax.rem(starts, SLOT_BASE),
        ],
        axis=1,
    ).astype(jnp.bfloat16)
    picked = jnp.dot(choose.astype(jnp.bfloat16), table, preferred_element_type=jnp.float32)
    picked = picked.astype(jnp.int32)
    owner_ends = picked[:, :blocks] * SLOT_BASE + picked[:, blocks : 2 * blocks]
    owner_starts = picked[:, 2 * blocks : 3 * blocks] * SLOT_BASE + picked[:, 3 * blocks :]
    window = jnp.sum((owner_ends <= offset[:, None]).astype(jnp.int32), axis=1)
    block_ids = jnp.arange(blocks, dtype=jnp.int32)
    block_pick = (window[:, None] == block_ids[None, :]).astype(jnp.int32)
    dest_slot = window * WINDOW_SLOTS + offset - jnp.sum(block_pick * owner_starts, axis=1)
    slot_code = dest_slot + 1
    tail_ids = jnp.arange(TAIL, dtype=jnp.int32)
    code_cols = jnp.where(
        tail_ids[None, :] == 0,
        lax.div(slot_code, SLOT_BASE)[:, None],
        jnp.where(tail_ids[None, :] == 1, lax.rem(slot_code, SLOT_BASE)[:, None], 0),
    ).astype(jnp.bfloat16)
    outgoing = place(send_hot, jnp.concatenate([rows_x, code_cols], axis=1))
    receiving = lax.all_to_all(
        outgoing.reshape(owner_count, capacity, model_dim + TAIL),
        "win",
        split_axis=0,
        concat_axis=0,
        tiled=True,
    ).reshape(buffer_rows, model_dim + TAIL)
    arrived = receiving[:, :model_dim]
    code_back = receiving[:, model_dim:].astype(jnp.int32)
    arrived_slot = code_back[:, 0] * SLOT_BASE + code_back[:, 1] - 1
    own_counts = lax.dynamic_index_in_dim(column_counts, win_index, 0, keepdims=False)
    slot_ids = jnp.arange(slots_all, dtype=jnp.int32)
    recv_hot = (slot_ids[:, None] == arrived_slot.reshape(1, buffer_rows)).astype(jnp.bfloat16)
    padded_x = place(recv_hot, arrived)
    column = jnp.arange(WINDOW_SLOTS, dtype=jnp.int32)
    usable_mask = column[None, :] < own_counts[:, None]
    first_pad = feed_forward(
        attention_block(padded_x, usable_mask, w_qkv_one, w_out_one), w_up, w_down
    )
    dilated_rows = lax.all_to_all(
        first_pad.reshape(blocks, dilation_stride, group_count, model_dim),
        "grp",
        split_axis=2,
        concat_axis=1,
        tiled=True,
    )
    owner_counts = lax.dynamic_index_in_dim(counts, win_index, 1, keepdims=False)
    k_ids = jnp.arange(dilation_stride, dtype=jnp.int32)
    valid_marks = (
        k_ids[None, None, :] * group_count + grp_index < jnp.transpose(owner_counts)[:, :, None]
    )
    block_count = dilated_rows.shape[0]
    flat_rows = dilated_rows.reshape(block_count * WINDOW_SLOTS, model_dim)
    mixed_rows = attention_block(
        flat_rows, valid_marks.reshape(block_count, WINDOW_SLOTS), w_qkv_two, w_out_two
    ).reshape(block_count, WINDOW_SLOTS, 1, model_dim)
    second_pad = lax.all_to_all(mixed_rows, "grp", split_axis=1, concat_axis=2, tiled=True).reshape(
        slots_all, model_dim
    )
    returning = place_back(recv_hot, second_pad)
    returned = lax.all_to_all(returning, "win", split_axis=0, concat_axis=0, tiled=True)
    encoded = place_back(send_hot, returned)
    return encoded.reshape(1, 1, local_points, model_dim)


def solution(mesh):
    return jax.shard_map(
        on_device,
        mesh=mesh,
        in_specs=(
            P("win", "grp", None, None),
            P("win", "grp", None),
            P(),
            P(),
            P(),
            P(),
            P(),
            P(),
            P(),
        ),
        out_specs=P("win", "grp", None, None),
        check_vma=False,
    )
```

profile of v0, /device:TPU:32, one launch (start us, length us, event | category | flops | bytes accessed | tf_op | source)
XLA Modules:
  0.0 162.5 jit_solution(15884425211801808277)
XLA Ops:
  3.6 3.1 %fusion.45 = bf16[1024,640]{1,0:T(8,128)(2,1)} fusion(s32[512]{0:T(512)S(1)} %get-tuple-element.17, bf16[512,128]{1,0:T(8,128)(2,1)S(1)} %select_convert_fusion, bf16[512,512]{1,0:T(8,128)(2,1)} %bitcast.182), kind=kOutput, calls=%fused_computation.61 | convolution fusion | flops 673579008 | bytes 1968128 | tf_op jit(solution)/shard_map/dot_general | solution.py:69
  6.8 11.4 %all-to-all-start = ((bf16[32,32,640]{2,1,0:T(8,128)(2,1)}), bf16[32,32,640]{2,1,0:T(8,128)(2,1)S(1)}, u32[]{:S(2)}, u32[]{:S(2)}) async-start(bf16[32,32,640]{2,1,0:T(8,128)(2,1)} %bitcast.169), calls=%async_computation | async-start | bytes 2621440 | tf_op jit(solution)/shard_map/all_to_all | solution.py:131
  18.1 2.6 %copy.77 = bf16[512,1536]{0,1:T(8,128)(2,1)} copy(bf16[512,1536]{1,0:T(8,128)(2,1)} %param.12) | data formatting | bytes 3145728 | tf_op args[3]
  21.0 2.6 %fusion.124 = (bf16[512,1,16,32]{0,3,2,1:T(8,128)(2,1)}, bf16[512,1,16,32]{0,3,2,1:T(8,128)(2,1)}, bf16[512,1,16,32]{0,3,2,1:T(8,128)(2,1)}) fusion(bf16[512,3,16,32]{0,3,2,1:T(8,128)(2,1)} %bitcast.158), kind=kLoop, calls=%fused_computation.181 | loop fusion | bytes 3145728 | tf_op jit(solution)/shard_map/slice | solution.py:36
  23.6 28.5 %all-to-all-done = bf16[32,32,640]{2,1,0:T(8,128)(2,1)S(1)} async-done(((bf16[32,32,640]{2,1,0:T(8,128)(2,1)}), bf16[32,32,640]{2,1,0:T(8,128)(2,1)S(1)}, u32[]{:S(2)}, u32[]{:S(2)}) %all-to-all-start) | async-done | bytes 1310752 | tf_op jit(solution)/shard_map/all_to_all | solution.py:131
  52.5 1.3 convert_reduce_fusion.1
  54.4 0.9 fusion.119
  57.3 1.3 fusion.72
  58.6 3.6 %fusion.125 = (f32[16,8,128]{2,1,0:T(8,128)S(1)}, f32[16,8,128,128]{2,3,1,0:T(8,128)S(1)}) fusion(f32[16,8,128,128]{2,3,1,0:T(8,128)S(1)} %fusion.72, pred[8,128]{1,0:T(8,128)(4,1)S(1)} %iota_compare_fusion.20), kind=kOutput, calls=%fused_computation.182 | output fusion | flops 12583039 | bytes 16843776 | tf_op jit(solution)/shard_map/sub | solution.py:46
  62.3 1.2 fusion.52
  64.9 7.4 %fusion.33 = bf16[1024,512]{1,0:T(8,128)(2,1)} fusion(bf16[1024,512]{1,0:T(8,128)(2,1)S(1)} %get-tuple-element.25, bf16[2048,512]{1,0:T(8,128)(2,1)S(1)} %copy-done, bf16[512,2048]{1,0:T(8,128)(2,1)} %param.14, f32[1024]{0:T(1024)S(1)} %add_rsqrt_fusion.1, f32[1024]{0:T(1024)S(1)} %broadcast_multiply_fusion.1), kind=kOutput, calls=%fused_computation.46 | convolution fusion | flops 4317511680 | bytes 6299648 | tf_op jit(solution)/shard_map/dot_general | solution.py:64
  72.3 2.5 %copy.83 = bf16[8,16,8,512]{3,1,0,2:T(8,128)(2,1)} copy(bf16[8,16,8,512]{3,2,1,0:T(8,128)(2,1)} %bitcast.170) | data formatting | bytes 2097152 | tf_op jit(solution)/shard_map/reshape | solution.py:151
  74.8 4.3 %all-to-all-start.1 = ((bf16[8,16,8,512]{3,1,0,2:T(8,128)(2,1)}), bf16[8,16,8,512]{3,1,0,2:T(8,128)(2,1)S(1)}, u32[]{:S(2)}, u32[]{:S(2)}) async-start(bf16[8,16,8,512]{3,1,0,2:T(8,128)(2,1)} %copy.83), calls=%async_computation.1 | async-start | bytes 2097152 | tf_op jit(solution)/shard_map/all_to_all | solution.py:150
  79.1 2.6 %copy.87 = bf16[512,1536]{0,1:T(8,128)(2,1)} copy(bf16[512,1536]{1,0:T(8,128)(2,1)} %param.16) | data formatting | bytes 3145728 | tf_op args[7]
  82.2 2.3 %fusion.123 = (bf16[512,1,16,32]{0,3,2,1:T(8,128)(2,1)S(1)}, bf16[512,1,16,32]{0,3,2,1:T(8,128)(2,1)S(1)}, bf16[512,1,16,32]{0,3,2,1:T(8,128)(2,1)}) fusion(bf16[512,3,16,32]{0,3,2,1:T(8,128)(2,1)} %bitcast.159), kind=kLoop, calls=%fused_computation.180 | loop fusion | bytes 3145728 | tf_op jit(solution)/shard_map/slice | solution.py:36
  84.5 10.5 %all-to-all-done.1 = bf16[8,16,8,512]{3,1,0,2:T(8,128)(2,1)S(1)} async-done(((bf16[8,16,8,512]{3,1,0,2:T(8,128)(2,1)}), bf16[8,16,8,512]{3,1,0,2:T(8,128)(2,1)S(1)}, u32[]{:S(2)}, u32[]{:S(2)}) %all-to-all-start.1) | async-done | bytes 1048608 | tf_op jit(solution)/shard_map/all_to_all | solution.py:150
  98.4 1.3 fusion.65
  99.8 3.5 %fusion.126 = (f32[16,8,128]{2,1,0:T(8,128)S(1)}, f32[16,8,128,128]{2,3,1,0:T(8,128)S(1)}) fusion(f32[16,8,128,128]{2,3,1,0:T(8,128)S(1)} %fusion.65, pred[8,128]{1,0:T(8,128)(4,1)S(1)} %broadcast_compare_fusion), kind=kOutput, calls=%fused_computation.183 | output fusion | flops 12583039 | bytes 16843776 | tf_op jit(solution)/shard_map/sub | solution.py:46
  103.2 1.2 fusion.53
  104.6 0.9 copy-done.8
  106.8 18.4 %all_to_all.41 = bf16[8,128,1,512]{3,0,2,1:T(8,128)(2,1)S(1)} all-to-all(bf16[8,128,1,512]{3,0,2,1:T(8,128)(2,1)S(1)} %copy.93), channel_id=1, replica_groups=mesh['win'=32,'grp'=8] {'grp'}, dimensions={1} | all-to-all | bytes 2097152 | tf_op jit(solution)/shard_map/all_to_all | solution.py:167
  126.2 1.3 fusion.47
  127.5 33.5 %all_to_all.42 = bf16[32,32,512]{2,1,0:T(8,128)(2,1)S(1)} all-to-all(bf16[32,32,512]{2,1,0:T(8,128)(2,1)S(1)} %bitcast.174), channel_id=1, replica_groups=mesh['win'=32,'grp'=8] {'win'}, dimensions={0} | all-to-all | bytes 2097152 | tf_op jit(solution)/shard_map/all_to_all | solution.py:171
  161.0 1.6 fusion.55
  (62 shorter events, 14.3 us)
Async XLA Ops:
  0.0 64.9 %copy-start = (bf16[2048,512]{1,0:T(8,128)(2,1)S(1)}, bf16[2048,512]{1,0:T(8,128)(2,1)}, u32[]{:S(2)}) copy-start(bf16[2048,512]{1,0:T(8,128)(2,1)} %param.15) | copy-start | bytes 6291460
  6.8 45.3 %all-to-all-start = ((bf16[32,32,640]{2,1,0:T(8,128)(2,1)}), bf16[32,32,640]{2,1,0:T(8,128)(2,1)S(1)}, u32[]{:S(2)}, u32[]{:S(2)}) async-start(bf16[32,32,640]{2,1,0:T(8,128)(2,1)} %bitcast.169), calls=%async_computation | async-start | bytes 2621440 | tf_op jit(solution)/shard_map/all_to_all | solution.py:131
  18.1 2.6 %copy-start.6 = (s32[8,32,8]{1,2,0:T(8,128)S(1)}, s32[8,32,8]{1,2,0:T(8,128)}, u32[]{:S(2)}) copy-start(s32[8,32,8]{1,2,0:T(8,128)} %param.11) | copy-start | bytes 24580
  52.5 1.9 %copy-start.5 = (bf16[512,1,16,32]{0,3,2,1:T(8,128)(2,1)S(1)}, bf16[512,1,16,32]{0,3,2,1:T(8,128)(2,1)}, u32[]{:S(2)}) copy-start(bf16[512,1,16,32]{0,3,2,1:T(8,128)(2,1)} %get-tuple-element.9) | copy-start | bytes 1572868
  54.4 1.0 copy-start.4
  55.3 1.1 copy-start.3
  62.3 1.2 copy-start.7
  74.8 20.2 %all-to-all-start.1 = ((bf16[8,16,8,512]{3,1,0,2:T(8,128)(2,1)}), bf16[8,16,8,512]{3,1,0,2:T(8,128)(2,1)S(1)}, u32[]{:S(2)}, u32[]{:S(2)}) async-start(bf16[8,16,8,512]{3,1,0,2:T(8,128)(2,1)} %copy.83), calls=%async_computation.1 | async-start | bytes 2097152 | tf_op jit(solution)/shard_map/all_to_all | solution.py:150
  95.0 1.2 copy-start.2
  104.4 1.1 copy-start.8
  127.5 35.1 %copy-start.1 = (bf16[2048,512]{1,0:T(8,128)(2,1)S(1)}, bf16[2048,512]{1,0:T(8,128)(2,1)}, u32[]{:S(2)}) copy-start(bf16[2048,512]{1,0:T(8,128)(2,1)} %param.15) | copy-start | bytes 6291460
where the time goes:
time: 163 us
  blocking collectives  51.9 us (32%)
  waiting for transfers between devices  39 us (24%)
  matrix products  26.7 us (16%)
  local copies, waits for them, and re-layouts  16.8 us (10%)
  starting transfers between devices  15.7 us (10%)
  other arithmetic  12.2 us (7%)
    all_to_all x1, blocking collectives, on_device(): lax.all_to_all(returning, 'win', split_axis=0, concat_axis=0, tiled=True)  33.5 us
    all_to_all x1, waiting for transfers between devices, on_device(): lax.all_to_all(outgoing.reshape(owner_count, capacity, model_dim + TAIL),...  28.5 us
    all_to_all x1, blocking collectives, on_device(): lax.all_to_all(mixed_rows, 'grp', split_axis=1, concat_axis=2, tiled=True)  18.4 us
    all_to_all x1, starting transfers between devices, on_device(): lax.all_to_all(outgoing.reshape(owner_count, capacity, model_dim + TAIL),...  11.4 us
    all_to_all x1, waiting for transfers between devices, on_device(): lax.all_to_all(first_pad.reshape(blocks, dilation_stride, group_count, mo...  10.5 us
    dot_general x1, matrix products, feed_forward(): jnp.dot(hidden, w_down, preferred_element_type=jnp.float32)  7.42 us
    sub x2, other arithmetic, attention_block(): weights = jnp.exp(scores - row_max)  7.12 us
    unnamed x20, local copies, waits for them, and re-layouts  6.35 us
  transfers between devices with their start and end apart: 2, of which 2 were waited for; matrix products, arithmetic and copies ran while one was open for 7% of the time, Pallas kernels for 0%

commit v1 on v0

--- a/solution.py
+++ b/solution.py
@@ -147,12 +147,20 @@
     first_pad = feed_forward(
         attention_block(padded_x, usable_mask, w_qkv_one, w_out_one), w_up, w_down
     )
-    dilated_rows = lax.all_to_all(
-        first_pad.reshape(blocks, dilation_stride, group_count, model_dim),
-        "grp",
-        split_axis=2,
-        concat_axis=1,
-        tiled=True,
+    dilated_rows = jnp.concatenate(
+        lax.all_to_all(
+            jnp.stack(
+                jnp.split(
+                    first_pad.reshape(blocks, dilation_stride, group_count, model_dim),
+                    lax.axis_size("grp"),
+                    axis=2,
+                )
+            ),
+            "grp",
+            0,
+            0,
+        ),
+        axis=1,
     )
     owner_counts = lax.dynamic_index_in_dim(counts, win_index, 1, keepdims=False)
     k_ids = jnp.arange(dilation_stride, dtype=jnp.int32)

time: 163 us -> 169 us (1.037)
  local copies, waits for them, and re-layouts: 16.8 us -> 22.4 us
    unnamed x20 -> x29, local copies, waits for them, and re-layouts: 6.35 us -> 11.1 us
    reshape x1 -> x0, local copies, waits for them, and re-layouts: 2.5 us -> none  [on_device(): first_pad.reshape(blocks, dilation_stride, group_count, model_dim)]
    split x0 -> x1, local copies, waits for them, and re-layouts: none -> 2.4 us  [on_device(): jnp.split(first_pad.reshape(blocks, dilation_stride, group_count, model_d...]
  transfers between devices with their start and end apart: 2 -> 2, of which waited for: 2 -> 2; matrix products, arithmetic and copies ran while one was open for 7% -> 6% of each run, Pallas kernels for 0% -> 0%
where the time goes in v1:
time: 169 us; the launch traced here: 168 us
  blocking collectives  51.9 us (31%)
  waiting for transfers between devices  39 us (23%)
  matrix products  26.3 us (16%)
  local copies, waits for them, and re-layouts  22.4 us (13%)
  starting transfers between devices  15.7 us (9%)
  other arithmetic  12.5 us (7%)
    all_to_all x1, blocking collectives, on_device(): lax.all_to_all(returning, 'win', split_axis=0, concat_axis=0, tiled=True)  33.5 us
    all_to_all x1, waiting for transfers between devices, on_device(): lax.all_to_all(outgoing.reshape(owner_count, capacity, model_dim + TAIL),...  28.5 us
    all_to_all x1, blocking collectives, on_device(): lax.all_to_all(mixed_rows, 'grp', split_axis=1, concat_axis=2, tiled=True)  18.4 us
    all_to_all x1, starting transfers between devices, on_device(): lax.all_to_all(outgoing.reshape(owner_count, capacity, model_dim + TAIL),...  11.4 us
    unnamed x29, local copies, waits for them, and re-layouts  11.1 us
    all_to_all x1, waiting for transfers between devices, on_device(): lax.all_to_all(jnp.stack(jnp.split(first_pad.reshape(blocks, dilation_str...  10.5 us
    sub x2, other arithmetic, attention_block(): weights = jnp.exp(scores - row_max)  7.12 us
    dot_general x1, matrix products, feed_forward(): jnp.dot(hidden, w_down, preferred_element_type=jnp.float32)  7 us
  transfers between devices with their start and end apart: 2, of which 2 were waited for; matrix products, arithmetic and copies ran while one was open for 6% of the time, Pallas kernels for 0%

profile of v1, /device:TPU:32, one launch (start us, length us, event | category | flops | bytes accessed | tf_op | source)
XLA Modules:
  0.0 168.0 jit_solution(4581859060134919895)
XLA Ops:
  3.6 3.1 %fusion.41 = bf16[1024,640]{1,0:T(8,128)(2,1)} fusion(s32[512]{0:T(512)S(1)} %get-tuple-element.25, bf16[512,128]{1,0:T(8,128)(2,1)S(1)} %select_convert_fusion, bf16[512,512]{1,0:T(8,128)(2,1)} %bitcast.202), kind=kOutput, calls=%fused_computation.58 | convolution fusion | flops 673579008 | bytes 1968128 | tf_op jit(solution)/shard_map/dot_general | solution.py:69
  6.8 11.4 %all-to-all-start = ((bf16[32,32,640]{2,1,0:T(8,128)(2,1)}), bf16[32,32,640]{2,1,0:T(8,128)(2,1)S(1)}, u32[]{:S(2)}, u32[]{:S(2)}) async-start(bf16[32,32,640]{2,1,0:T(8,128)(2,1)} %bitcast.191), calls=%async_computation | async-start | bytes 2621440 | tf_op jit(solution)/shard_map/all_to_all | solution.py:131
  18.1 2.6 %copy.80 = bf16[512,1536]{0,1:T(8,128)(2,1)} copy(bf16[512,1536]{1,0:T(8,128)(2,1)} %param.12) | data formatting | bytes 3145728 | tf_op args[3]
  21.0 2.6 %fusion.129 = (bf16[512,1,16,32]{0,3,2,1:T(8,128)(2,1)}, bf16[512,1,16,32]{0,3,2,1:T(8,128)(2,1)}, bf16[512,1,16,32]{0,3,2,1:T(8,128)(2,1)}) fusion(bf16[512,3,16,32]{0,3,2,1:T(8,128)(2,1)} %bitcast.179), kind=kLoop, calls=%fused_computation.194 | loop fusion | bytes 3145728 | tf_op jit(solution)/shard_map/slice | solution.py:36
  23.6 28.5 %all-to-all-done = bf16[32,32,640]{2,1,0:T(8,128)(2,1)S(1)} async-done(((bf16[32,32,640]{2,1,0:T(8,128)(2,1)}), bf16[32,32,640]{2,1,0:T(8,128)(2,1)S(1)}, u32[]{:S(2)}, u32[]{:S(2)}) %all-to-all-start) | async-done | bytes 1310752 | tf_op jit(solution)/shard_map/all_to_all | solution.py:131
  52.5 1.3 convert_reduce_fusion.1
  54.4 0.9 fusion.124
  56.4 0.9 fusion.122
  57.3 1.3 fusion.69
  58.6 3.6 %fusion.131 = (f32[16,8,128]{2,1,0:T(8,128)S(1)}, f32[16,8,128,128]{2,3,1,0:T(8,128)S(1)}) fusion(f32[16,8,128,128]{2,3,1,0:T(8,128)S(1)} %fusion.69, pred[8,128]{1,0:T(8,128)(4,1)S(1)} %iota_compare_fusion.20), kind=kOutput, calls=%fused_computation.196 | output fusion | flops 12583039 | bytes 16843776 | tf_op jit(solution)/shard_map/sub | solution.py:46
  62.3 1.2 fusion.49
  65.3 7.0 %fusion.33 = bf16[1024,512]{1,0:T(8,128)(2,1)S(1)} fusion(bf16[1024,512]{1,0:T(8,128)(2,1)} %copy-done.3, bf16[2048,512]{1,0:T(8,128)(2,1)S(1)} %copy-done, bf16[512,2048]{1,0:T(8,128)(2,1)} %param.14, f32[1024]{0:T(1024)S(1)} %add_rsqrt_fusion.1, f32[1024]{0:T(1024)S(1)} %broadcast_multiply_fusion.1), kind=kOutput, calls=%fused_computation.46 | convolution fusion | flops 4317511680 | bytes 6299648 | tf_op jit(solution)/shard_map/dot_general | solution.py:64
  72.3 2.4 %fusion.130 = (bf16[8,16,1,512]{3,2,1,0:T(2,128)(2,1)S(1)}, bf16[8,16,1,512]{3,2,1,0:T(2,128)(2,1)S(1)}, bf16[8,16,1,512]{3,2,1,0:T(2,128)(2,1)S(1)}, bf16[8,16,...) fusion(bf16[8,16,8,512]{3,2,1,0:T(8,128)(2,1)S(1)} %bitcast.181), kind=kLoop, calls=%fused_computation.195 | loop fusion | bytes 2097152 | tf_op jit(solution)/shard_map/split | solution.py:153
  80.1 4.3 %all-to-all-start.1 = ((bf16[8,8,16,1,512]{4,2,1,3,0:T(8,128)(2,1)}), bf16[8,8,16,1,512]{4,2,1,3,0:T(8,128)(2,1)S(1)}, u32[]{:S(2)}, u32[]{:S(2)}) async-start(bf16[8,8,16,1,512]{4,2,1,3,0:T(8,128)(2,1)} %fusion.88), calls=%async_computation.1 | async-start | bytes 2097152 | tf_op jit(solution)/shard_map/all_to_all | solution.py:151
  84.4 2.6 %copy.98 = bf16[512,1536]{0,1:T(8,128)(2,1)} copy(bf16[512,1536]{1,0:T(8,128)(2,1)} %param.16) | data formatting | bytes 3145728 | tf_op args[7]
  87.5 2.3 %fusion.128 = (bf16[512,1,16,32]{0,3,2,1:T(8,128)(2,1)S(1)}, bf16[512,1,16,32]{0,3,2,1:T(8,128)(2,1)S(1)}, bf16[512,1,16,32]{0,3,2,1:T(8,128)(2,1)}) fusion(bf16[512,3,16,32]{0,3,2,1:T(8,128)(2,1)} %bitcast.180), kind=kLoop, calls=%fused_computation.193 | loop fusion | bytes 3145728 | tf_op jit(solution)/shard_map/slice | solution.py:36
  89.8 10.5 %all-to-all-done.1 = bf16[8,8,16,1,512]{4,2,1,3,0:T(8,128)(2,1)S(1)} async-done(((bf16[8,8,16,1,512]{4,2,1,3,0:T(8,128)(2,1)}), bf16[8,8,16,1,512]{4,2,1,3,0:T(8,128)(2,1)S(1)}, u32[]{:S(2)}, u32[]{:S(2)}) %all-to-all-start.1) | async-done | bytes 1048608 | tf_op jit(solution)/shard_map/all_to_all | solution.py:151
  105.0 1.3 fusion.62
  106.3 3.5 %fusion.132 = (f32[16,8,128]{2,1,0:T(8,128)S(1)}, f32[16,8,128,128]{2,3,1,0:T(8,128)S(1)}) fusion(f32[16,8,128,128]{2,3,1,0:T(8,128)S(1)} %fusion.62, pred[8,128]{1,0:T(8,128)(4,1)S(1)} %broadcast_compare_fusion), kind=kOutput, calls=%fused_computation.197 | output fusion | flops 12583039 | bytes 16843776 | tf_op jit(solution)/shard_map/sub | solution.py:46
  109.8 1.2 fusion.50
  112.4 18.4 %all_to_all.37 = bf16[8,128,1,512]{3,0,2,1:T(8,128)(2,1)S(1)} all-to-all(bf16[8,128,1,512]{3,0,2,1:T(8,128)(2,1)S(1)} %copy.104), channel_id=1, replica_groups=mesh['win'=32,'grp'=8] {'grp'}, dimensions={1} | all-to-all | bytes 2097152 | tf_op jit(solution)/shard_map/all_to_all | solution.py:175
  131.7 1.3 fusion.44
  133.0 33.5 %all_to_all.38 = bf16[32,32,512]{2,1,0:T(8,128)(2,1)S(1)} all-to-all(bf16[32,32,512]{2,1,0:T(8,128)(2,1)S(1)} %bitcast.194), channel_id=1, replica_groups=mesh['win'=32,'grp'=8] {'win'}, dimensions={0} | all-to-all | bytes 2097152 | tf_op jit(solution)/shard_map/all_to_all | solution.py:179
  166.5 1.6 fusion.52
  (74 shorter events, 20.4 us)
Async XLA Ops:
  0.0 65.3 %copy-start = (bf16[2048,512]{1,0:T(8,128)(2,1)S(1)}, bf16[2048,512]{1,0:T(8,128)(2,1)}, u32[]{:S(2)}) copy-start(bf16[2048,512]{1,0:T(8,128)(2,1)} %param.15) | copy-start | bytes 6291460
  6.8 45.3 %all-to-all-start = ((bf16[32,32,640]{2,1,0:T(8,128)(2,1)}), bf16[32,32,640]{2,1,0:T(8,128)(2,1)S(1)}, u32[]{:S(2)}, u32[]{:S(2)}) async-start(bf16[32,32,640]{2,1,0:T(8,128)(2,1)} %bitcast.191), calls=%async_computation | async-start | bytes 2621440 | tf_op jit(solution)/shard_map/all_to_all | solution.py:131
  18.1 2.6 %copy-start.7 = (s32[8,32,8]{1,2,0:T(8,128)S(1)}, s32[8,32,8]{1,2,0:T(8,128)}, u32[]{:S(2)}) copy-start(s32[8,32,8]{1,2,0:T(8,128)} %param.11) | copy-start | bytes 24580
  52.5 1.9 %copy-start.6 = (bf16[512,1,16,32]{0,3,2,1:T(8,128)(2,1)S(1)}, bf16[512,1,16,32]{0,3,2,1:T(8,128)(2,1)}, u32[]{:S(2)}) copy-start(bf16[512,1,16,32]{0,3,2,1:T(8,128)(2,1)} %get-tuple-element.9) | copy-start | bytes 1572868
  54.4 1.0 copy-start.5
  55.3 1.1 copy-start.4
  62.3 1.2 copy-start.8
  64.3 1.0 copy-start.3
  80.1 20.2 %all-to-all-start.1 = ((bf16[8,8,16,1,512]{4,2,1,3,0:T(8,128)(2,1)}), bf16[8,8,16,1,512]{4,2,1,3,0:T(8,128)(2,1)S(1)}, u32[]{:S(2)}, u32[]{:S(2)}) async-start(bf16[8,8,16,1,512]{4,2,1,3,0:T(8,128)(2,1)} %fusion.88), calls=%async_computation.1 | async-start | bytes 2097152 | tf_op jit(solution)/shard_map/all_to_all | solution.py:151
  101.1 1.0 copy-start.2
  109.8 1.2 copy-start.9
  133.0 35.1 %copy-start.1 = (bf16[2048,512]{1,0:T(8,128)(2,1)S(1)}, bf16[2048,512]{1,0:T(8,128)(2,1)}, u32[]{:S(2)}) copy-start(bf16[2048,512]{1,0:T(8,128)(2,1)} %param.15) | copy-start | bytes 6291460
